TPU v7x, 32 devices: a whole 2x2x4 slice. The times are simulated.
32 devices in a mesh: groups: 2 (over y), filt: 4 (over z), patch: 4 (over x, core).
Axes of the slice: x: 2, y: 2, z: 4, core: 2. Of those that a mesh axis runs over, the one named last changes fastest.
Arguments:
- activations: bfloat16 [8, 256, 4, 128, 128], P(('groups', 'patch'), None, None, 'filt'), parts along dimension 0, may hold values from -6 to 6
- filters: bfloat16 [3, 3, 3, 256, 256], replicated, may hold values from -0.078125 to 0.078125
- bias: bfloat16 [256], replicated, may hold values from -3 to 3
- cotangent: bfloat16 [8, 256, 4, 128, 128], P(('groups', 'patch'), None, None, 'filt'), parts along dimension 0, may hold values from -6 to 6
Outputs:
- output: bfloat16 [8, 256, 4, 128, 128], P(('groups', 'patch'), None, None, 'filt'), parts along dimension 0
- filter_grad: float32 [6, 3, 3, 256, 256], P('groups', None, None, None, 'filt'), parts along dimension 0
- bias_grad: float32 [512], P(('groups', 'filt')), parts along dimension 0
There are 2 independent parts, one for each index of `groups`. A program takes and returns all parts, laid end to end along the dimension named above; an argument that names none is the same for every part. Nothing has to cross between parts.
All inputs are finite; a program needn't handle non-finite values.
Results may differ from a plain program's by a relative error of at most 0.001.
Values may be sent and summed in bfloat16 or wider, within the bound.
No kernel may reach another device: no remote copies, remote signals or barrier semaphores. Data moves between devices by JAX's collectives and lax.ppermute only.
A program may use at most 640 MiB of HBM per device.

v0:
```python
import math

import jax
import jax.numpy as jnp
from jax import lax
from jax.sharding import PartitionSpec as P


def padded_2(cells, sides, width):
    for axis, dim in sides:
        count = lax.axis_size(axis)
        ends = count - 1
        head = lax.slice_in_dim(cells, 0, width, axis=dim)
        tail = lax.slice_in_dim(cells, cells.shape[dim] - width, cells.shape[dim], axis=dim)
        cells = jnp.concatenate(
            [
                lax.ppermute(tail, axis, [(i, (i + 1) % count) for i in range(ends)]),
                cells,
                lax.ppermute(head, axis, [((i + 1) % count, i) for i in range(ends)]),
            ],
            axis=dim,
        )
    return cells


def local(activations, filters, bias, cotangent):
    count, channels, depth, rows, width = activations.shape
    owned = channels // lax.axis_size("filt")
    scale = 1.0 / math.sqrt(
        count * lax.axis_size("patch") * depth * rows * lax.axis_size("filt") * width
    )
    rimmed = padded_2(activations, (("filt", 3),), 1)
    padded = jnp.pad(rimmed, ((0, 0), (0, 0), (1, 1), (0, 0), (1, 1)))
    accum = jnp.zeros((count, channels, depth, rows, width), jnp.float32)
    terms = []
    for tap_a in range(3):
        for tap_b in range(3):
            for tap_c in range(3):
                window = padded[
                    :, :, tap_a : tap_a + depth, tap_b : tap_b + rows, tap_c : tap_c + width
                ]
                accum = accum + jnp.einsum(
                    "pidhw,io->podhw",
                    window,
                    filters[tap_a, tap_b, tap_c],
                    preferred_element_type=jnp.float32,
                )
                terms.append(
                    jnp.einsum(
                        "pidhw,podhw->oi", window, cotangent, preferred_element_type=jnp.float32
                    )
                )
    output = (accum + bias.astype(jnp.float32)[None, :, None, None, None]).astype(jnp.bfloat16)
    grads_all = jnp.stack(terms, axis=1)
    bias_all = jnp.sum(cotangent.astype(jnp.float32), axis=(0, 2, 3, 4))
    grads, bias_part = (
        lax.psum_scatter(grads_all, "filt", scatter_dimension=0, tiled=True),
        lax.psum_scatter(bias_all, "filt", scatter_dimension=0, tiled=True),
    )
    grads, bias_part = lax.psum((grads, bias_part), "patch")
    filter_grad = jnp.transpose(grads.reshape(owned, 3, 3, 3, channels), (1, 2, 3, 4, 0)) * scale
    return (output, filter_grad, bias_part * scale)


def solution(mesh):
    return jax.shard_map(
        local,
        mesh=mesh,
        in_specs=(
            P(("groups", "patch"), None, None, "filt", None),
            P(),
            P(),
            P(("groups", "patch"), None, None, "filt", None),
        ),
        out_specs=(
            P(("groups", "patch"), None, None, "filt", None),
            P("groups", None, None, None, "filt"),
            P(("groups", "filt")),
        ),
        check_vma=False,
    )
```

profile of v0, /device:TPU:0, one launch (start us, length us, event | category | flops | bytes accessed | tf_op | source)
XLA Modules:
  0.0 898.5 jit_solution(8330301384658841170)
XLA Ops:
  7.2 13.7 %copy.138 = bf16[1,256,4,32,128]{1,4,3,2,0:T(8,128)(2,1)} copy(bf16[1,256,4,32,128]{4,3,2,1,0:T(8,128)(2,1)} %param.4) | data formatting | bytes 16777216 | tf_op args[0]
  22.1 5.1 collective-permute-start
  28.6 18.9 %fusion.59 = f32[256,4,32,128]{0,3,2,1:T(8,128)} fusion(bf16[256,4,32,128]{3,2,1,0:T(8,128)(2,1)} %bitcast.798, bf16[3,3,3,256,256]{4,3,2,1,0:T(8,128)(2,1)} %param.5), kind=kOutput, calls=%fused_computation.106 | convolution fusion | flops 2147483648 | bytes 25296896 | tf_op jit(solution)/shard_map/pidhw,io->podhw/dot_general | solution.py:42
  51.0 13.7 %all-reduce.1 = f32[256]{0:T(256)S(1)} all-reduce(f32[256]{0:T(256)S(1)} %convert_reduce_fusion), channel_id=3, replica_groups=mesh['groups'=2,'filt'=4,'patch'=4] {'filt'}, use_global_device_ids=true, to_apply=%region_3.4.clone | all-reduce | flops 256 | bytes 2048
  64.8 6.0 psum.15
  71.3 20.6 %select_maximum_fusion = bf16[1,256,6,34,130]{1,4,3,2,0:T(8,128)(2,1)S(1)} fusion(bf16[1,256,4,1,128]{1,4,3,2,0:T(8,128)(2,1)} %collective-permute-done.1, bf16[1,256,4,32,128]{1,4,3,2,0:T(8,128)(2,1)} %copy.138, bf16[1,256,4,1,128]{1,4,3,2,0:T(8,128)(2,1)S(1)} %collective-permute-done), kind=kLoop, calls=%fused_computation.24 | loop fusion | flops 128993280 | bytes 22491136 | tf_op jit(solution)/shard_map/concatenate | solution.py:15
  91.9 9.7 %fusion.11 = f32[4,32,128,256]{3,2,1,0:T(8,128)} fusion(bf16[1,256,6,34,130]{1,4,3,2,0:T(8,128)(2,1)S(1)} %select_maximum_fusion, bf16[3,3,3,256,256]{4,3,2,1,0:T(8,128)(2,1)} %param.5), kind=kOutput, calls=%fused_computation.58 | convolution fusion | flops 2147483648 | bytes 25296896 | tf_op jit(solution)/shard_map/pidhw,io->podhw/dot_general | solution.py:42
  101.6 9.2 %fusion.13 = f32[4,32,128,256]{3,2,1,0:T(8,128)} fusion(bf16[1,256,6,34,130]{1,4,3,2,0:T(8,128)(2,1)S(1)} %select_maximum_fusion, bf16[3,3,3,256,256]{4,3,2,1,0:T(8,128)(2,1)} %param.5), kind=kOutput, calls=%fused_computation.60 | convolution fusion | flops 2147483648 | bytes 25296896 | tf_op jit(solution)/shard_map/pidhw,io->podhw/dot_general | solution.py:42
  110.8 9.0 fusion.17
  119.7 9.0 %fusion.19 = f32[4,32,128,256]{3,2,1,0:T(8,128)} fusion(bf16[1,256,6,34,130]{1,4,3,2,0:T(8,128)(2,1)S(1)} %select_maximum_fusion, bf16[3,3,3,256,256]{4,3,2,1,0:T(8,128)(2,1)} %param.5), kind=kOutput, calls=%fused_computation.66 | convolution fusion | flops 2147483648 | bytes 25296896 | tf_op jit(solution)/shard_map/pidhw,io->podhw/dot_general | solution.py:42
  128.7 9.0 fusion.23
  137.7 9.2 %fusion.25 = f32[4,32,128,256]{3,2,1,0:T(8,128)} fusion(bf16[1,256,6,34,130]{1,4,3,2,0:T(8,128)(2,1)S(1)} %select_maximum_fusion, bf16[3,3,3,256,256]{4,3,2,1,0:T(8,128)(2,1)} %param.5), kind=kOutput, calls=%fused_computation.72 | convolution fusion | flops 2147483648 | bytes 25296896 | tf_op jit(solution)/shard_map/pidhw,io->podhw/dot_general | solution.py:42
  146.9 9.0 fusion.29
  155.9 9.1 %fusion.33 = f32[4,32,128,256]{3,2,1,0:T(8,128)} fusion(bf16[1,256,6,34,130]{1,4,3,2,0:T(8,128)(2,1)S(1)} %select_maximum_fusion, bf16[3,3,3,256,256]{4,3,2,1,0:T(8,128)(2,1)} %param.5), kind=kOutput, calls=%fused_computation.80 | convolution fusion | flops 2147483648 | bytes 25296896 | tf_op jit(solution)/shard_map/pidhw,io->podhw/dot_general | solution.py:42
  164.9 9.1 %fusion.37 = f32[4,32,128,256]{3,2,1,0:T(8,128)} fusion(bf16[1,256,6,34,130]{1,4,3,2,0:T(8,128)(2,1)S(1)} %select_maximum_fusion, bf16[3,3,3,256,256]{4,3,2,1,0:T(8,128)(2,1)} %param.5), kind=kOutput, calls=%fused_computation.84 | convolution fusion | flops 2147483648 | bytes 25296896 | tf_op jit(solution)/shard_map/pidhw,io->podhw/dot_general | solution.py:42
  174.0 9.0 fusion.41
  182.9 9.2 %fusion.43 = f32[4,32,128,256]{3,2,1,0:T(8,128)} fusion(bf16[1,256,6,34,130]{1,4,3,2,0:T(8,128)(2,1)S(1)} %select_maximum_fusion, bf16[3,3,3,256,256]{4,3,2,1,0:T(8,128)(2,1)} %param.5), kind=kOutput, calls=%fused_computation.90 | convolution fusion | flops 2147483648 | bytes 25296896 | tf_op jit(solution)/shard_map/pidhw,io->podhw/dot_general | solution.py:42
  192.2 9.0 fusion.47
  201.2 13.6 %fusion.135 = f32[256,27,256]{0,2,1:T(8,128)} fusion(bf16[1,256,6,34,130]{1,4,3,2,0:T(8,128)(2,1)S(1)} %select_maximum_fusion, bf16[256,4,32,128]{3,2,1,0:T(8,128)(2,1)} %bitcast.800), kind=kOutput, calls=%fused_computation.166 | convolution fusion | flops 2147483648 | bytes 17039360 | tf_op jit(solution)/shard_map/pidhw,podhw->oi/dot_general | solution.py:49
  214.8 14.0 %fusion.133 = f32[256,27,256]{0,2,1:T(8,128)} fusion(f32[256,27,256]{0,2,1:T(8,128)} %fusion.135, bf16[1,256,6,34,130]{1,4,3,2,0:T(8,128)(2,1)S(1)} %select_maximum_fusion, bf16[256,4,32,128]{3,2,1,0:T(8,128)(2,1)} %bitcast.801), kind=kOutput, calls=%fused_computation.164 | convolution fusion | flops 2147483648 | bytes 17039360 | tf_op jit(solution)/shard_map/pidhw,podhw->oi/dot_general | solution.py:49
  228.8 13.8 %fusion.131 = f32[256,27,256]{0,2,1:T(8,128)} fusion(f32[256,27,256]{0,2,1:T(8,128)} %fusion.133, bf16[1,256,6,34,130]{1,4,3,2,0:T(8,128)(2,1)S(1)} %select_maximum_fusion, bf16[256,4,32,128]{3,2,1,0:T(8,128)(2,1)} %bitcast.802), kind=kOutput, calls=%fused_computation.162 | convolution fusion | flops 2147483648 | bytes 17039360 | tf_op jit(solution)/shard_map/pidhw,podhw->oi/dot_general | solution.py:49
  242.6 13.9 %fusion.129 = f32[256,27,256]{0,2,1:T(8,128)} fusion(f32[256,27,256]{0,2,1:T(8,128)} %fusion.131, bf16[1,256,6,34,130]{1,4,3,2,0:T(8,128)(2,1)S(1)} %select_maximum_fusion, bf16[256,4,32,128]{3,2,1,0:T(8,128)(2,1)} %bitcast.803), kind=kOutput, calls=%fused_computation.160 | convolution fusion | flops 2147483648 | bytes 17039360 | tf_op jit(solution)/shard_map/pidhw,podhw->oi/dot_general | solution.py:49
  256.5 14.0 %fusion.127 = f32[256,27,256]{0,2,1:T(8,128)} fusion(f32[256,27,256]{0,2,1:T(8,128)} %fusion.129, bf16[1,256,6,34,130]{1,4,3,2,0:T(8,128)(2,1)S(1)} %select_maximum_fusion, bf16[256,4,32,128]{3,2,1,0:T(8,128)(2,1)} %bitcast.804), kind=kOutput, calls=%fused_computation.158 | convolution fusion | flops 2147483648 | bytes 17039360 | tf_op jit(solution)/shard_map/pidhw,podhw->oi/dot_general | solution.py:49
  270.5 13.6 %fusion.125 = f32[256,27,256]{0,2,1:T(8,128)} fusion(f32[256,27,256]{0,2,1:T(8,128)} %fusion.127, bf16[1,256,6,34,130]{1,4,3,2,0:T(8,128)(2,1)S(1)} %select_maximum_fusion, bf16[256,4,32,128]{3,2,1,0:T(8,128)(2,1)} %bitcast.805), kind=kOutput, calls=%fused_computation.156 | convolution fusion | flops 2147483648 | bytes 17039360 | tf_op jit(solution)/shard_map/pidhw,podhw->oi/dot_general | solution.py:49
  284.2 13.8 %fusion.123 = f32[256,27,256]{0,2,1:T(8,128)} fusion(f32[256,27,256]{0,2,1:T(8,128)} %fusion.125, bf16[1,256,6,34,130]{1,4,3,2,0:T(8,128)(2,1)S(1)} %select_maximum_fusion, bf16[256,4,32,128]{3,2,1,0:T(8,128)(2,1)} %bitcast.806), kind=kOutput, calls=%fused_computation.154 | convolution fusion | flops 2147483648 | bytes 17039360 | tf_op jit(solution)/shard_map/pidhw,podhw->oi/dot_general | solution.py:49
  298.0 13.8 %fusion.121 = f32[256,27,256]{0,2,1:T(8,128)} fusion(f32[256,27,256]{0,2,1:T(8,128)} %fusion.123, bf16[1,256,6,34,130]{1,4,3,2,0:T(8,128)(2,1)S(1)} %select_maximum_fusion, bf16[256,4,32,128]{3,2,1,0:T(8,128)(2,1)} %bitcast.807), kind=kOutput, calls=%fused_computation.152 | convolution fusion | flops 2147483648 | bytes 17039360 | tf_op jit(solution)/shard_map/pidhw,podhw->oi/dot_general | solution.py:49
  311.9 14.0 %fusion.119 = f32[256,27,256]{0,2,1:T(8,128)} fusion(f32[256,27,256]{0,2,1:T(8,128)} %fusion.121, bf16[1,256,6,34,130]{1,4,3,2,0:T(8,128)(2,1)S(1)} %select_maximum_fusion, bf16[256,4,32,128]{3,2,1,0:T(8,128)(2,1)} %bitcast.808), kind=kOutput, calls=%fused_computation.150 | convolution fusion | flops 2147483648 | bytes 17039360 | tf_op jit(solution)/shard_map/pidhw,podhw->oi/dot_general | solution.py:49
  325.9 13.7 %fusion.117 = f32[256,27,256]{0,2,1:T(8,128)} fusion(f32[256,27,256]{0,2,1:T(8,128)} %fusion.119, bf16[1,256,6,34,130]{1,4,3,2,0:T(8,128)(2,1)S(1)} %select_maximum_fusion, bf16[256,4,32,128]{3,2,1,0:T(8,128)(2,1)} %bitcast.809), kind=kOutput, calls=%fused_computation.148 | convolution fusion | flops 2147483648 | bytes 17039360 | tf_op jit(solution)/shard_map/pidhw,podhw->oi/dot_general | solution.py:49
  339.6 16.3 %fusion.79 = f32[256,27,256]{0,2,1:T(8,128)} fusion(f32[256,27,256]{0,2,1:T(8,128)} %fusion.117, bf16[1,256,4,32,128]{1,4,3,2,0:T(8,128)(2,1)} %copy.138, bf16[1,256,4,1,128]{1,4,3,2,0:T(8,128)(2,1)S(1)} %copy-done.3, bf16[256,4,32,128]{3,2,1,0:T(8,128)(2,1)} %bitcast.810), kind=kOutput, calls=%fused_computation.116 | convolution fusion | flops 2151677952 | bytes 17301504 | tf_op jit(solution)/shard_map/pidhw,podhw->oi/dot_general | solution.py:49
  355.9 13.8 %fusion.115 = f32[256,27,256]{0,2,1:T(8,128)} fusion(f32[256,27,256]{0,2,1:T(8,128)} %fusion.79, bf16[1,256,6,34,130]{1,4,3,2,0:T(8,128)(2,1)S(1)} %select_maximum_fusion, bf16[256,4,32,128]{3,2,1,0:T(8,128)(2,1)} %bitcast.811), kind=kOutput, calls=%fused_computation.146 | convolution fusion | flops 2147483648 | bytes 17039360 | tf_op jit(solution)/shard_map/pidhw,podhw->oi/dot_general | solution.py:49
  369.7 14.1 %fusion.113 = f32[256,27,256]{0,2,1:T(8,128)} fusion(f32[256,27,256]{0,2,1:T(8,128)} %fusion.115, bf16[1,256,6,34,130]{1,4,3,2,0:T(8,128)(2,1)S(1)} %select_maximum_fusion, bf16[256,4,32,128]{3,2,1,0:T(8,128)(2,1)} %bitcast.812), kind=kOutput, calls=%fused_computation.144 | convolution fusion | flops 2147483648 | bytes 17039360 | tf_op jit(solution)/shard_map/pidhw,podhw->oi/dot_general | solution.py:49
  383.8 15.7 %fusion.85 = f32[256,27,256]{0,2,1:T(8,128)} fusion(f32[256,27,256]{0,2,1:T(8,128)} %fusion.113, bf16[256,4,32,128]{3,2,1,0:T(8,128)(2,1)} %bitcast.799, bf16[256,4,32,128]{3,2,1,0:T(8,128)(2,1)} %bitcast.813), kind=kOutput, calls=%fused_computation.118 | convolution fusion | flops 2147483648 | bytes 17039360 | tf_op jit(solution)/shard_map/pidhw,podhw->oi/dot_general | solution.py:49
  399.5 13.6 %fusion.111 = f32[256,27,256]{0,2,1:T(8,128)} fusion(f32[256,27,256]{0,2,1:T(8,128)} %fusion.85, bf16[1,256,6,34,130]{1,4,3,2,0:T(8,128)(2,1)S(1)} %select_maximum_fusion, bf16[256,4,32,128]{3,2,1,0:T(8,128)(2,1)} %bitcast.814), kind=kOutput, calls=%fused_computation.142 | convolution fusion | flops 2147483648 | bytes 17039360 | tf_op jit(solution)/shard_map/pidhw,podhw->oi/dot_general | solution.py:49
  413.2 13.8 %fusion.109 = f32[256,27,256]{0,2,1:T(8,128)} fusion(f32[256,27,256]{0,2,1:T(8,128)} %fusion.111, bf16[1,256,6,34,130]{1,4,3,2,0:T(8,128)(2,1)S(1)} %select_maximum_fusion, bf16[256,4,32,128]{3,2,1,0:T(8,128)(2,1)} %bitcast.815), kind=kOutput, calls=%fused_computation.140 | convolution fusion | flops 2147483648 | bytes 17039360 | tf_op jit(solution)/shard_map/pidhw,podhw->oi/dot_general | solution.py:49
  427.0 16.6 %fusion.73 = f32[256,27,256]{0,2,1:T(8,128)} fusion(f32[256,27,256]{0,2,1:T(8,128)} %fusion.109, bf16[1,256,4,1,128]{1,4,3,2,0:T(8,128)(2,1)} %collective-permute-done.1, bf16[1,256,4,32,128]{1,4,3,2,0:T(8,128)(2,1)} %copy.138, bf16[256,4,32,128]{3,2,1,0:T(8,128)(2,1)} %bitcast.816), kind=kOutput, calls=%fused_computation.114 | convolution fusion | flops 2151677952 | bytes 17301504 | tf_op jit(solution)/shard_map/pidhw,podhw->oi/dot_general | solution.py:49
  443.6 13.8 %fusion.107 = f32[256,27,256]{0,2,1:T(8,128)} fusion(f32[256,27,256]{0,2,1:T(8,128)} %fusion.73, bf16[1,256,6,34,130]{1,4,3,2,0:T(8,128)(2,1)S(1)} %select_maximum_fusion, bf16[256,4,32,128]{3,2,1,0:T(8,128)(2,1)} %bitcast.817), kind=kOutput, calls=%fused_computation.138 | convolution fusion | flops 2147483648 | bytes 17039360 | tf_op jit(solution)/shard_map/pidhw,podhw->oi/dot_general | solution.py:49
  457.4 13.7 %fusion.105 = f32[256,27,256]{0,2,1:T(8,128)} fusion(f32[256,27,256]{0,2,1:T(8,128)} %fusion.107, bf16[1,256,6,34,130]{1,4,3,2,0:T(8,128)(2,1)S(1)} %select_maximum_fusion, bf16[256,4,32,128]{3,2,1,0:T(8,128)(2,1)} %bitcast.818), kind=kOutput, calls=%fused_computation.136 | convolution fusion | flops 2147483648 | bytes 17039360 | tf_op jit(solution)/shard_map/pidhw,podhw->oi/dot_general | solution.py:49
  471.0 13.9 %fusion.103 = f32[256,27,256]{0,2,1:T(8,128)} fusion(f32[256,27,256]{0,2,1:T(8,128)} %fusion.105, bf16[1,256,6,34,130]{1,4,3,2,0:T(8,128)(2,1)S(1)} %select_maximum_fusion, bf16[256,4,32,128]{3,2,1,0:T(8,128)(2,1)} %bitcast.819), kind=kOutput, calls=%fused_computation.134 | convolution fusion | flops 2147483648 | bytes 17039360 | tf_op jit(solution)/shard_map/pidhw,podhw->oi/dot_general | solution.py:49
  484.9 14.0 %fusion.101 = f32[256,27,256]{0,2,1:T(8,128)} fusion(f32[256,27,256]{0,2,1:T(8,128)} %fusion.103, bf16[1,256,6,34,130]{1,4,3,2,0:T(8,128)(2,1)S(1)} %select_maximum_fusion, bf16[256,4,32,128]{3,2,1,0:T(8,128)(2,1)} %bitcast.820), kind=kOutput, calls=%fused_computation.132 | convolution fusion | flops 2147483648 | bytes 17039360 | tf_op jit(solution)/shard_map/pidhw,podhw->oi/dot_general | solution.py:49
  498.9 13.8 %fusion.99 = f32[256,27,256]{0,2,1:T(8,128)} fusion(f32[256,27,256]{0,2,1:T(8,128)} %fusion.101, bf16[1,256,6,34,130]{1,4,3,2,0:T(8,128)(2,1)S(1)} %select_maximum_fusion, bf16[256,4,32,128]{3,2,1,0:T(8,128)(2,1)} %bitcast.821), kind=kOutput, calls=%fused_computation.130 | convolution fusion | flops 2147483648 | bytes 17039360 | tf_op jit(solution)/shard_map/pidhw,podhw->oi/dot_general | solution.py:49
  512.8 13.8 %fusion.97 = f32[256,27,256]{0,2,1:T(8,128)} fusion(f32[256,27,256]{0,2,1:T(8,128)} %fusion.99, bf16[1,256,6,34,130]{1,4,3,2,0:T(8,128)(2,1)S(1)} %select_maximum_fusion, bf16[256,4,32,128]{3,2,1,0:T(8,128)(2,1)} %bitcast.822), kind=kOutput, calls=%fused_computation.128 | convolution fusion | flops 2147483648 | bytes 17039360 | tf_op jit(solution)/shard_map/pidhw,podhw->oi/dot_general | solution.py:49
  526.6 13.6 %fusion.95 = f32[256,27,256]{0,2,1:T(8,128)} fusion(f32[256,27,256]{0,2,1:T(8,128)} %fusion.97, bf16[1,256,6,34,130]{1,4,3,2,0:T(8,128)(2,1)S(1)} %select_maximum_fusion, bf16[256,4,32,128]{3,2,1,0:T(8,128)(2,1)} %bitcast.823), kind=kOutput, calls=%fused_computation.126 | convolution fusion | flops 2147483648 | bytes 17039360 | tf_op jit(solution)/shard_map/pidhw,podhw->oi/dot_general | solution.py:49
  540.2 14.1 %fusion.93 = f32[256,27,256]{0,2,1:T(8,128)} fusion(f32[256,27,256]{0,2,1:T(8,128)} %fusion.95, bf16[1,256,6,34,130]{1,4,3,2,0:T(8,128)(2,1)S(1)} %select_maximum_fusion, bf16[256,4,32,128]{3,2,1,0:T(8,128)(2,1)} %bitcast.824), kind=kOutput, calls=%fused_computation.124 | convolution fusion | flops 2147483648 | bytes 17039360 | tf_op jit(solution)/shard_map/pidhw,podhw->oi/dot_general | solution.py:49
  554.3 13.8 %fusion.91 = f32[256,27,256]{0,2,1:T(8,128)} fusion(f32[256,27,256]{0,2,1:T(8,128)} %fusion.93, bf16[1,256,6,34,130]{1,4,3,2,0:T(8,128)(2,1)S(1)} %select_maximum_fusion, bf16[256,4,32,128]{3,2,1,0:T(8,128)(2,1)} %bitcast.825), kind=kOutput, calls=%fused_computation.122 | convolution fusion | flops 2147483648 | bytes 17039360 | tf_op jit(solution)/shard_map/pidhw,podhw->oi/dot_general | solution.py:49
  568.1 14.0 %fusion.89 = f32[256,27,256]{0,2,1:T(8,128)} fusion(f32[256,27,256]{0,2,1:T(8,128)} %fusion.91, bf16[1,256,6,34,130]{1,4,3,2,0:T(8,128)(2,1)S(1)} %select_maximum_fusion, bf16[256,4,32,128]{3,2,1,0:T(8,128)(2,1)} %bitcast.826), kind=kOutput, calls=%fused_computation.120 | convolution fusion | flops 2147483648 | bytes 17039360 | tf_op jit(solution)/shard_map/pidhw,podhw->oi/dot_general | solution.py:49
  582.1 10.4 %copy.201 = f32[256,27,256]{2,1,0:T(8,128)} copy(f32[256,27,256]{0,2,1:T(8,128)} %fusion.89) | data formatting | bytes 14155776 | tf_op jit(solution)/shard_map/stack | solution.py:54
  592.7 11.5 %fusion.64 = f32[4,32,128,256]{3,2,1,0:T(8,128)} fusion(bf16[1,256,4,32,128]{1,4,3,2,0:T(8,128)(2,1)} %copy.138, bf16[1,256,4,1,128]{1,4,3,2,0:T(8,128)(2,1)} %copy-done.2, bf16[3,3,3,256,256]{4,3,2,1,0:T(8,128)(2,1)S(1)} %copy-done.1), kind=kOutput, calls=%fused_computation.110 | convolution fusion | flops 2151677952 | bytes 25559040 | tf_op jit(solution)/shard_map/pidhw,io->podhw/dot_general | solution.py:42
  604.2 11.8 %fusion.68 = f32[4,32,128,256]{3,2,1,0:T(8,128)} fusion(bf16[1,256,4,1,128]{1,4,3,2,0:T(8,128)(2,1)} %collective-permute-done.1, bf16[1,256,4,32,128]{1,4,3,2,0:T(8,128)(2,1)} %copy.138, bf16[3,3,3,256,256]{4,3,2,1,0:T(8,128)(2,1)S(1)} %copy-done.1), kind=kOutput, calls=%fused_computation.112 | convolution fusion | flops 2151677952 | bytes 25559040 | tf_op jit(solution)/shard_map/pidhw,io->podhw/dot_general | solution.py:42
  616.0 8.1 fusion.49
  624.1 8.1 fusion.53
  632.2 8.1 fusion.55
  640.3 8.3 fusion.15
  648.6 8.2 fusion.21
  656.8 8.2 fusion.27
  665.0 8.3 fusion.31
  673.3 8.2 fusion.35
  681.5 8.4 fusion.39
  689.9 8.1 fusion.45
  698.0 8.1 fusion.51
  706.1 29.7 %reduce-scatter.2.cloned.1.call-done = f32[64,27,256]{2,1,0:T(8,128)} async-done(((f32[256,27,256]{2,1,0:T(8,128)}), f32[64,27,256]{2,1,0:T(8,128)}) %reduce-scatter.2.cloned.1.call-update) | async-done | bytes 1769488 | tf_op jit(solution)/shard_map/reduce_scatter | solution.py:57
  735.8 3.8 copy.202
  739.7 134.4 %fusion.61 = bf16[1,256,4,32,128]{1,4,3,2,0:T(8,128)(2,1)} fusion(f32[256]{0:T(256)S(1)} %copy-done.4, bf16[1,256,6,34,130]{1,4,3,2,0:T(8,128)(2,1)} %copy-done, f32[4,32,128,256]{3,2,1,0:T(8,128)} %fusion.55, f32[4,32,128,256]{3,2,1,0:T(8,128)} %fusion.53, f32[4,32,128,256]{3,2,1,0:T(8,128)} %fusion.51, f32[4,32,128,256]{3,2,1,0:T(8,128)} %fusion.49, ...), kind=kOutput, calls=%fused_computation.108 | convolution fusion | flops 2264924160 | bytes 453116928 | tf_op jit(solution)/shard_map/pidhw,io->podhw/dot_general | solution.py:42
  874.0 14.5 %copy.203 = bf16[1,256,4,32,128]{4,3,2,1,0:T(8,128)(2,1)} copy(bf16[1,256,4,32,128]{1,4,3,2,0:T(8,128)(2,1)} %fusion.61) | data formatting | bytes 16777216
  888.6 2.9 broadcast_multiply_fusion
  (42 shorter events, 6.1 us)
Async XLA Ops:
  7.2 728.7 %reduce-scatter.2.cloned.1.call-start = ((), (), s32[]{:S(2)}) async-start(), calls=%async_computation.1 | async-start | bytes 10485760 | tf_op jit(solution)/shard_map/reduce_scatter | solution.py:57
  20.9 26.5 %slice-start.4 = ((s8[8388608]{0:T(1024)(128)(4,1)}), s8[4194304]{0:T(1024)(128)(4,1)S(1)}, s32[]{:S(2)}) async-start(s8[8388608]{0:T(1024)(128)(4,1)} %bitcast.827), calls=%async_computation.7 | async-start | bytes 8388608
  22.1 49.1 %collective-permute-start = (bf16[1,256,4,1,128]{1,4,3,2,0:T(8,128)(2,1)S(1)}, bf16[1,256,4,1,128]{1,4,3,2,0:T(8,128)(2,1)S(1)}, u32[]{:S(2)}, u32[]{:S(2)}) collective-permute-start(bf16[1,256,4,1,128]{1,4,3,2,0:T(8,128)(2,1)S(1)} %get-tuple-element.12), channel_id=1, source_target_pairs={{0,4},{4,8},{8,12},{1,5},{5,9},{9,13},{2,6},{6,10},{10,14},{3,7},{... | collective-permute-start | bytes 786440 | tf_op jit(solution)/shard_map/ppermute | solution.py:17
  27.2 44.0 %collective-permute-start.1 = (bf16[1,256,4,1,128]{1,4,3,2,0:T(8,128)(2,1)S(1)}, bf16[1,256,4,1,128]{1,4,3,2,0:T(8,128)(2,1)}, u32[]{:S(2)}, u32[]{:S(2)}) collective-permute-start(bf16[1,256,4,1,128]{1,4,3,2,0:T(8,128)(2,1)S(1)} %get-tuple-element.13), channel_id=1, source_target_pairs={{4,0},{8,4},{12,8},{5,1},{9,5},{13,9},{6,2},{10,6},{14,10},{7,3},{... | collective-permute-start | bytes 786440 | tf_op jit(solution)/shard_map/ppermute | solution.py:19
  28.5 18.9 %slice-start.5 = ((s8[8388608]{0:T(1024)(128)(4,1)}), s8[4194304]{0:T(1024)(128)(4,1)S(1)}, s32[]{:S(2)}) async-start(s8[8388608]{0:T(1024)(128)(4,1)} %bitcast.827), calls=%async_computation.8 | async-start | bytes 8388608
  47.5 1.7 copy-start.5
  47.5 2.3 copy-start.6
  71.3 20.6 %copy-start.2 = (bf16[1,256,4,1,128]{1,4,3,2,0:T(8,128)(2,1)}, bf16[1,256,4,1,128]{1,4,3,2,0:T(8,128)(2,1)S(1)}, u32[]{:S(2)}) copy-start(bf16[1,256,4,1,128]{1,4,3,2,0:T(8,128)(2,1)S(1)} %collective-permute-done) | copy-start | bytes 786436
  91.9 476.2 %copy-start = (bf16[1,256,6,34,130]{1,4,3,2,0:T(8,128)(2,1)}, bf16[1,256,6,34,130]{1,4,3,2,0:T(8,128)(2,1)S(1)}, u32[]{:S(2)}) copy-start(bf16[1,256,6,34,130]{1,4,3,2,0:T(8,128)(2,1)S(1)} %select_maximum_fusion) | copy-start | bytes 40734724
  325.9 13.7 %copy-start.3 = (bf16[1,256,4,1,128]{1,4,3,2,0:T(8,128)(2,1)S(1)}, bf16[1,256,4,1,128]{1,4,3,2,0:T(8,128)(2,1)}, u32[]{:S(2)}) copy-start(bf16[1,256,4,1,128]{1,4,3,2,0:T(8,128)(2,1)} %copy-done.2) | copy-start | bytes 786436
  582.1 10.5 %copy-start.1 = (bf16[3,3,3,256,256]{4,3,2,1,0:T(8,128)(2,1)S(1)}, bf16[3,3,3,256,256]{4,3,2,1,0:T(8,128)(2,1)}, u32[]{:S(2)}) copy-start(bf16[3,3,3,256,256]{4,3,2,1,0:T(8,128)(2,1)} %param.5) | copy-start | bytes 10616836
  592.6 296.0 %all-reduce.4.cloned.1.call-start = ((), (), s32[]{:S(2)}) async-start(), calls=%async_computation.2 | async-start | bytes 3538944 | tf_op jit(solution)/shard_map/psum | solution.py:60
  592.7 23.3 %slice-start = ((s8[14204928]{0:T(1024)(128)(4,1)}), s8[4194304]{0:T(1024)(128)(4,1)S(1)}, s32[]{:S(2)}) async-start(s8[14204928]{0:T(1024)(128)(4,1)} %bitcast.796), calls=%async_computation.3 | async-start | bytes 8388608
  592.7 23.3 %slice-start.1 = ((s8[14204928]{0:T(1024)(128)(4,1)}), s8[4194304]{0:T(1024)(128)(4,1)S(1)}, s32[]{:S(2)}) async-start(s8[14204928]{0:T(1024)(128)(4,1)} %bitcast.796), calls=%async_computation.4 | async-start | bytes 8388608
  604.2 11.8 %slice-start.2 = ((s8[14204928]{0:T(1024)(128)(4,1)}), s8[4194304]{0:T(1024)(128)(4,1)S(1)}, s32[]{:S(2)}) async-start(s8[14204928]{0:T(1024)(128)(4,1)} %bitcast.796), calls=%async_computation.5 | async-start | bytes 8388608
  604.2 11.8 %slice-start.3 = ((s8[14204928]{0:T(1024)(128)(4,1)}), s8[1622016]{0:T(1024)(128)(4,1)S(1)}, s32[]{:S(2)}) async-start(s8[14204928]{0:T(1024)(128)(4,1)} %bitcast.796), calls=%async_computation.6 | async-start | bytes 3244032
  698.0 41.7 %copy-start.4 = (f32[256]{0:T(256)S(1)}, f32[256]{0:T(256)}, u32[]{:S(2)}) copy-start(f32[256]{0:T(256)} %convert_element_type.14) | copy-start | bytes 3076
Sparse Core Ops, SparseCore 0:
  592.7 143.0 reduce-scatter.1
  739.8 46.6 all-reduce.3
where the time goes:
time: 909 us; the launch traced here: 898 us
  matrix products  757 us (83%)
  local copies, waits for them, and re-layouts  44.4 us (5%)
  waiting for transfers between devices  29.8 us (3%)
  other arithmetic  26.2 us (3%)
  blocking collectives  19.7 us (2%)
  between operations  15.1 us (2%)
    dot_general x27, matrix products, local(): jnp.einsum('pidhw,podhw->oi', window, cotangent, preferred_element_type=j...  381 us
    dot_general x27, matrix products, local(): jnp.einsum('pidhw,io->podhw', window, filters[tap_a, tap_b, tap_c], prefe...  376 us
    reduce_scatter x1, waiting for transfers between devices, local(): lax.psum_scatter(grads_all, 'filt', scatter_dimension=0, tiled=True)  29.7 us
    unnamed x30, local copies, waits for them, and re-layouts  28.9 us
    concatenate x1, other arithmetic, padded_2(): jnp.concatenate([lax.ppermute(tail, axis, [(i, (i + 1) % count) for i in...  20.6 us
  transfers between devices with their start and end apart: 4, of which 1 were waited for; matrix products, arithmetic and copies ran while one was open for 32% of the time, Pallas kernels for 0%

commit v1 on v0

v1 whole, which is shorter than its diff:
```python
import functools
import math

import jax
import jax.numpy as jnp
from jax import lax
from jax.experimental import pallas as pl
from jax.experimental.pallas import tpu as pltpu
from jax.sharding import PartitionSpec as P


def padded_2(cells, sides, width):
    for axis, dim in sides:
        count = lax.axis_size(axis)
        ends = count - 1
        head = lax.slice_in_dim(cells, 0, width, axis=dim)
        tail = lax.slice_in_dim(cells, cells.shape[dim] - width, cells.shape[dim], axis=dim)
        cells = jnp.concatenate(
            [
                lax.ppermute(tail, axis, [(i, (i + 1) % count) for i in range(ends)]),
                cells,
                lax.ppermute(head, axis, [((i + 1) % count, i) for i in range(ends)]),
            ],
            axis=dim,
        )
    return cells


def _wgrad_kernel(depth, lanes, x_ref, g_ref, o_ref):
    e = pl.program_id(0)
    a = pl.program_id(1)
    d = e + 1 - a

    @pl.when((e == 0) & (a == 0))
    def _():
        o_ref[...] = jnp.zeros_like(o_ref)

    @pl.when((d >= 0) & (d < depth))
    def _():
        g = g_ref[0]
        for b in range(3):
            win = x_ref[0, :, pl.ds(128 * b, lanes)]
            o_ref[a, b] += lax.dot_general(
                win, g, (((1,), (1,)), ((), ())), preferred_element_type=jnp.float32
            )


def wgrad(xc, gp):
    depth, rows3, lanes_h = xc.shape
    _, chans, lanes = gp.shape
    cost = pl.CostEstimate(
        flops=2 * 9 * depth * 3 * rows3 * chans * lanes // 3 * 3,
        bytes_accessed=xc.size * 2 + gp.size * 2 * 3 + 9 * rows3 * chans * 4,
        transcendentals=0,
    )
    return pl.pallas_call(
        functools.partial(_wgrad_kernel, depth, lanes),
        grid=(depth, 3),
        in_specs=[
            pl.BlockSpec((1, rows3, lanes_h), lambda e, a: (e, 0, 0)),
            pl.BlockSpec(
                (1, chans, lanes),
                lambda e, a: (jnp.clip(e + 1 - a, 0, depth - 1), 0, 0),
            ),
        ],
        out_specs=pl.BlockSpec((3, 3, rows3, chans), lambda e, a: (0, 0, 0, 0)),
        out_shape=jax.ShapeDtypeStruct((3, 3, rows3, chans), jnp.float32),
        compiler_params=pltpu.CompilerParams(
            dimension_semantics=("arbitrary", "arbitrary"),
            vmem_limit_bytes=60 * 1024 * 1024,
        ),
        cost_estimate=cost,
    )(xc, gp)


def local(activations, filters, bias, cotangent):
    count, channels, depth, rows, width = activations.shape
    n_filt = lax.axis_size("filt")
    n_patch = lax.axis_size("patch")
    owned = channels // n_filt
    piece = owned // n_patch
    scale = 1.0 / math.sqrt(count * n_patch * depth * rows * n_filt * width)
    rimmed = padded_2(activations, (("filt", 3),), 1)
    accum = lax.conv_general_dilated(
        rimmed,
        filters,
        window_strides=(1, 1, 1),
        padding=((1, 1), (0, 0), (1, 1)),
        dimension_numbers=("NCDHW", "DHWIO", "NCDHW"),
        preferred_element_type=jnp.float32,
    )
    output = (accum + bias.astype(jnp.float32)[None, :, None, None, None]).astype(jnp.bfloat16)
    wide = jnp.pad(rimmed[0], ((0, 0), (0, 0), (0, 0), (1, 1)))
    shifts = jnp.stack([wide[..., c : c + width] for c in range(3)])
    xc = jnp.transpose(shifts, (2, 0, 1, 3, 4)).reshape(depth, 3 * channels, (rows + 2) * width)
    gp = cotangent[0].reshape(n_filt, n_patch, piece, depth, rows, width)
    gp = jnp.transpose(gp, (3, 1, 0, 2, 4, 5)).reshape(depth, channels, rows * width)
    grads_all = wgrad(xc, gp)
    grads = jnp.transpose(grads_all.reshape(27 * channels, channels), (1, 0))
    grads = grads.reshape(n_patch * n_filt, piece * 27, channels)
    grads = lax.psum_scatter(grads, ("patch", "filt"), scatter_dimension=0, tiled=True)
    grads = lax.all_gather(grads, "patch", axis=0, tiled=True)
    grads = grads.reshape(owned, 3, 3, 3, channels)
    filter_grad = jnp.transpose(grads, (1, 2, 3, 4, 0)) * scale
    bias_all = jnp.sum(cotangent.astype(jnp.float32), axis=(0, 2, 3, 4))
    bias_part = lax.psum_scatter(bias_all, "filt", scatter_dimension=0, tiled=True)
    bias_part = lax.psum(bias_part, "patch")
    return (output, filter_grad, bias_part * scale)


def solution(mesh):
    return jax.shard_map(
        local,
        mesh=mesh,
        in_specs=(
            P(("groups", "patch"), None, None, "filt", None),
            P(),
            P(),
            P(("groups", "patch"), None, None, "filt", None),
        ),
        out_specs=(
            P(("groups", "patch"), None, None, "filt", None),
            P("groups", None, None, None, "filt"),
            P(("groups", "filt")),
        ),
        check_vma=False,
    )
```

time: 909 us -> 453 us (0.50)
  matrix products: 757 us -> 70.4 us
  local copies, waits for them, and re-layouts: 44.4 us -> 208 us
  Pallas kernels: 0 us -> 61.4 us
  other arithmetic: 26.2 us -> 40.9 us
    dot_general x54 -> x0, matrix products: 757 us -> none  [the longest x27 381 us: local(): jnp.einsum('pidhw,podhw->oi', window, cotangent, preferred_element_type=j...]
    reshape x0 -> x5, local copies, waits for them, and re-layouts: none -> 103 us  [the longest x2 72.5 us: local(): jnp.transpose(shifts, (2, 0, 1, 3, 4))]
    conv_general_dilated x0 -> x1, matrix products: none -> 70.4 us  [local(): lax.conv_general_dilated(rimmed, filters, window_strides=(1, 1, 1), paddi...]
    pallas_call x0 -> x1, Pallas kernels: none -> 61.4 us  [wgrad(): pl.pallas_call(functools.partial(_wgrad_kernel, depth, lanes), grid=(dept...]
    transpose x0 -> x1, other arithmetic: none -> 21.2 us  [local(): jnp.transpose(shifts, (2, 0, 1, 3, 4))]
    concatenate x1 -> x0, other arithmetic: 20.6 us -> none  [padded_2(): jnp.concatenate([lax.ppermute(tail, axis, [(i, (i + 1) % count) for i in...]
    convert_element_type x0 -> x2, local copies, waits for them, and re-layouts: none -> 16.7 us  [local(): (accum + bias.astype(jnp.float32)[None, :, None, None, None]).astype(jnp....]
    squeeze x0 -> x1, other arithmetic: none -> 11.3 us  [local(): wide = jnp.pad(rimmed[0], ((0, 0), (0, 0), (0, 0), (1, 1)))]
  transfers between devices with their start and end apart: 4 -> 4, of which waited for: 1 -> 1; matrix products, arithmetic and copies ran while one was open for 32% -> 38% of each run, Pallas kernels for 0% -> 0%
where the time goes in v1:
time: 453 us; the launch traced here: 450 us
  local copies, waits for them, and re-layouts  208 us (46%)
  matrix products  70.4 us (16%)
  Pallas kernels  61.4 us (14%)
  other arithmetic  40.9 us (9%)
  waiting for transfers between devices  30.8 us (7%)
  blocking collectives  15.8 us (3%)
  between operations  14.8 us (3%)
  starting transfers between devices  7.85 us (2%)
    reshape x2, local copies, waits for them, and re-layouts, local(): jnp.transpose(shifts, (2, 0, 1, 3, 4))  72.5 us
    conv_general_dilated x1, matrix products, local(): lax.conv_general_dilated(rimmed, filters, window_strides=(1, 1, 1), paddi...  70.4 us
    pallas_call x1, Pallas kernels, wgrad(): pl.pallas_call(functools.partial(_wgrad_kernel, depth, lanes), grid=(dept...  61.4 us
    unnamed x15, local copies, waits for them, and re-layouts  38.9 us
    reduce_scatter x1, waiting for transfers between devices, local(): lax.psum_scatter(grads, ('patch', 'filt'), scatter_dimension=0, tiled=True)  30.8 us
    transpose x1, other arithmetic, local(): jnp.transpose(shifts, (2, 0, 1, 3, 4))  21.2 us
    convert_element_type x2, local copies, waits for them, and re-layouts, local(): (accum + bias.astype(jnp.float32)[None, :, None, None, None]).astype(jnp....  16.7 us
    reshape x1, local copies, waits for them, and re-layouts, local(): jnp.transpose(gp, (3, 1, 0, 2, 4, 5)).reshape(depth, channels, rows * width)  13.3 us
  transfers between devices with their start and end apart: 4, of which 1 were waited for; matrix products, arithmetic and copies ran while one was open for 38% of the time, Pallas kernels for 0%

profile of v1, /device:TPU:0, one launch (start us, length us, event | category | flops | bytes accessed | tf_op | source)
XLA Modules:
  0.0 449.6 jit_solution(2608055722259567013)
XLA Ops:
  7.2 0.0 copy-start
  7.2 0.0 reduce-scatter.2.cloned.1.call-start
  7.2 3.2 fusion.18
  10.4 0.7 copy.33
  11.2 1.3 collective-permute-start.1
  12.5 0.7 copy.32
  13.2 6.3 %collective-permute-start = (bf16[1,256,4,1,128]{4,1,3,2,0:T(8,128)(2,1)}, bf16[1,256,4,1,128]{4,1,3,2,0:T(8,128)(2,1)}, u32[]{:S(2)}, u32[]{:S(2)}) collective-permute-start(bf16[1,256,4,1,128]{4,1,3,2,0:T(8,128)(2,1)} %copy.32), channel_id=1, source_target_pairs={{0,4},{4,8},{8,12},{1,5},{5,9},{9,13},{2,6},{6,10},{10,14},{3,7},{... | collective-permute-start | bytes 786440 | tf_op jit(solution)/shard_map/ppermute | solution.py:20
  19.5 9.4 %copy.36 = bf16[4,4,16,4,32,128]{5,4,2,0,1,3:T(8,128)(2,1)} copy(bf16[4,4,16,4,32,128]{5,4,3,2,1,0:T(8,128)(2,1)} %bitcast.37) | data formatting | bytes 16777216 | tf_op jit(solution)/shard_map/reshape;squeeze | solution.py:96
  28.9 13.3 %reshape.26.g_ref = bf16[4,256,4096]{2,1,0:T(8,128)(2,1)} reshape(bf16[4,4,4,16,32,128]{5,4,3,2,1,0:T(8,128)(2,1)} %bitcast.38) | data formatting | bytes 16777216 | tf_op jit(solution)/shard_map/reshape | solution.py:97
  42.1 0.0 collective-permute-done.1
  42.1 1.4 copy.21
  43.5 0.0 collective-permute-done
  43.5 1.4 copy.20
  44.9 11.3 %fusion.13 = (bf16[256,4,34,128]{3,2,1,0:T(8,128)(2,1)S(1)}, bf16[256,4,34,1,128]{4,2,1,0,3:T(8,128)(2,1)}) fusion(bf16[1,256,4,1,128]{4,3,2,1,0:T(2,128)(2,1)S(1)} %copy.21, bf16[1,256,4,32,128]{4,3,2,1,0:T(8,128)(2,1)} %param.4, bf16[1,256,4,1,128]{4,3,2,1,0:T(2,128)(2,1)S(1)} %copy.20), kind=kLoop, calls=%fused_computation.19 | loop fusion | flops 26738688 | bytes 26738688 | tf_op jit(solution)/shard_map/squeeze | solution.py:93
  56.2 9.9 %fusion.8 = (bf16[1,256,4,34,128]{4,3,2,1,0:T(8,128)(2,1)}, bf16[1,256,4,34,128]{4,3,2,1,0:T(8,128)(2,1)}) fusion(bf16[256,4,34,128]{3,2,1,0:T(8,128)(2,1)S(1)} %get-tuple-element.11), kind=kLoop, calls=%fused_computation.13 | loop fusion | bytes 26738688 | tf_op jit(solution)/shard_map/stack | solution.py:94
  66.1 21.2 %maximum_bitcast_fusion = bf16[4,3,256,34,128]{4,3,0,2,1:T(8,128)(2,1)} fusion(bf16[1,256,4,34,128]{4,3,2,1,0:T(8,128)(2,1)} %get-tuple-element.10, bf16[1,256,4,1,128]{4,3,2,1,0:T(2,128)(2,1)S(1)} %copy.21, bf16[1,256,4,32,128]{4,3,2,1,0:T(8,128)(2,1)} %param.4, bf16[1,256,4,1,128]{4,3,2,1,0:T(2,128)(2,1)S(1)} %copy.20, ...), kind=kLoop, calls=%fused_computation | loop fusion | flops 133693440 | bytes 53477376 | tf_op jit(solution)/shard_map/transpose | solution.py:95
  87.3 48.8 %reshape.41 = bf16[4,768,4352]{2,0,1:T(4,128)(2,1)} reshape(bf16[4,3,256,34,128]{4,3,0,2,1:T(8,128)(2,1)} %maximum_bitcast_fusion) | data formatting | bytes 53477376 | tf_op jit(solution)/shard_map/reshape | solution.py:95
  136.1 23.7 %copy.31.x_ref = bf16[4,768,4352]{2,1,0:T(8,128)(2,1)} copy(bf16[4,768,4352]{2,0,1:T(4,128)(2,1)} %reshape.41) | data formatting | bytes 53477376 | tf_op jit(solution)/shard_map/reshape | solution.py:95
  159.8 61.4 %shard_map.67 = f32[3,3,768,256]{3,2,1,0:T(8,128)} custom-call(bf16[4,768,4352]{2,1,0:T(8,128)(2,1)} %copy.31.x_ref, bf16[4,256,4096]{2,1,0:T(8,128)(2,1)} %reshape.26.g_ref), custom_call_target="tpu_custom_call" | custom-call | flops 173946175488 | bytes 58982400 | tf_op jit(solution)/shard_map/pallas_call | solution.py:56
  221.1 8.5 %copy.28 = f32[6912,256]{0,1:T(8,128)} copy(f32[6912,256]{1,0:T(8,128)} %bitcast.41) | data formatting | bytes 14155776 | tf_op jit(solution)/shard_map/reshape | solution.py:99
  229.6 0.0 copy-start.1
  229.6 0.0 copy-start.2
  229.6 8.5 %reshape.28 = f32[16,432,256]{2,1,0:T(8,128)} reshape(f32[256,6912]{1,0:T(8,128)} %bitcast.39) | data formatting | bytes 14155776 | tf_op jit(solution)/shard_map/reshape | solution.py:100
  238.1 0.0 reduce-scatter.2.cloned.1.call-update
  238.1 0.3 all-gather.2.cloned.1.call-start
  238.4 0.0 copy-done.1
  238.4 0.0 copy-done.2
  238.4 0.6 dynamic-slice
  239.7 5.0 %convert_reduce_fusion = f32[256]{0:T(256)S(1)} fusion(bf16[1,256,4,32,128]{4,3,2,1,0:T(8,128)(2,1)} %param.7), kind=kLoop, calls=%fused_computation.6 | loop fusion | flops 8388352 | bytes 8389632 | tf_op jit(solution)/shard_map/reduce_sum | solution.py:105
  244.7 10.2 %all-reduce.1 = f32[256]{0:T(256)S(1)} all-reduce(f32[256]{0:T(256)S(1)} %convert_reduce_fusion), channel_id=3, replica_groups=mesh['groups'=2,'filt'=4,'patch'=4] {'filt'}, use_global_device_ids=true, to_apply=%region_2.3.clone | all-reduce | flops 256 | bytes 2048
  254.9 0.1 dynamic-slice.1
  255.0 5.6 %psum.7 = f32[64]{0:T(128)S(1)} all-reduce(f32[64]{0:T(128)S(1)} %dynamic-slice.1), channel_id=1, replica_groups=mesh['groups'=2,'filt'=4,'patch'=4] {'patch'}, use_global_device_ids=true, to_apply=%region_3.4 | all-reduce | flops 64 | bytes 512 | tf_op jit(solution)/shard_map/psum | solution.py:107
  260.6 0.5 broadcast_multiply_fusion.1
  261.1 16.7 %copy.34 = bf16[256,4,34,1,128]{0,1,4,2,3:T(4,128)(2,1)} copy(bf16[256,4,34,1,128]{4,2,1,0,3:T(8,128)(2,1)} %get-tuple-element.12) | data formatting | bytes 17825792
  277.9 9.1 %pad.5.clone = bf16[256,4,34,1,136]{0,1,4,2,3:T(4,128)(2,1)} pad(bf16[256,4,34,1,128]{0,1,4,2,3:T(4,128)(2,1)} %copy.34, bf16[]{:T(256)} %constant.3.clone.1), padding=0_0x0_0x0_0x0_0x1_7 | pad | bytes 18382850 | tf_op jit(solution)/shard_map/concatenate | solution.py:18
  286.9 0.0 copy-start.3
  286.9 8.6 %copy.24 = bf16[256,4,34,1,8,17]{0,4,5,2,1,3:T(8,128)(2,1)} copy(bf16[256,4,34,1,8,17]{0,1,5,4,2,3:T(4,128)(2,1)} %bitcast.35) | data formatting | bytes 18939904 | tf_op jit(solution)/shard_map/conv_general_dilated | solution.py:84
  295.5 2.5 slice.19
  298.0 30.8 %reduce-scatter.2.cloned.1.call-done = f32[1,432,256]{2,1,0:T(8,128)} async-done(((f32[16,432,256]{2,1,0:T(8,128)}), f32[1,432,256]{2,1,0:T(8,128)}) %reduce-scatter.2.cloned.1.call-update) | async-done | bytes 442384 | tf_op jit(solution)/shard_map/reduce_scatter | solution.py:101
  328.8 0.0 all-gather.2.cloned.1.call-update
  328.8 0.0 copy-done
  328.9 0.0 copy-done.3
  328.9 70.4 %add_convert_fusion = bf16[4,32,8,17,256]{4,2,3,1,0:T(8,128)(2,1)} fusion(f32[256]{0:T(256)S(1)} %convert_element_type.11, pred[8,17]{0,1:T(8,128)(4,1)S(1)} %copy-done.3, bf16[3,3,3,256,256]{4,3,2,1,0:T(8,128)(2,1)S(1)} %copy-done, bf16[256,4,34,1,7,2]{0,4,5,2,1,3:T(8,128)(2,1)} %slice.19, bf16[256,4,34,1,8,17]{0,4,5,2,1,3:T(8,128)(2,1)} %copy.24), kind=kOutput, calls=%fused_computation.5 | convolution fusion | flops 51383402496 | bytes 22897800 | tf_op jit(solution)/shard_map/conv_general_dilated | solution.py:84
  399.2 9.1 %copy.25 = bf16[4,32,8,17,256]{4,1,3,2,0:T(8,128)(2,1)} copy(bf16[4,32,8,17,256]{4,2,3,1,0:T(8,128)(2,1)} %add_convert_fusion) | data formatting | bytes 17825792 | tf_op jit(solution)/shard_map/convert_element_type | solution.py:92
  408.3 7.6 %slice_bitcast_fusion = bf16[1,256,4,32,128]{1,3,4,2,0:T(8,128)(2,1)} fusion(bf16[4,32,1,136,256]{4,1,3,0,2:T(8,128)(2,1)} %bitcast.36), kind=kLoop, calls=%fused_computation.16 | loop fusion | bytes 16777216 | tf_op jit(solution)/shard_map/convert_element_type | solution.py:92
  416.0 16.9 %copy.29 = bf16[1,256,4,32,128]{4,3,2,1,0:T(8,128)(2,1)} copy(bf16[1,256,4,32,128]{1,3,4,2,0:T(8,128)(2,1)} %slice_bitcast_fusion) | data formatting | bytes 16777216
  432.8 0.0 all-gather.2.cloned.1.call-done
  432.8 2.8 broadcast_multiply_fusion
  435.6 4.0 mul.20
  439.6 3.2 copy.30
  (1 shorter events, 0.0 us)
Async XLA Ops:
  7.2 321.7 %copy-start = (bf16[3,3,3,256,256]{4,3,2,1,0:T(8,128)(2,1)S(1)}, bf16[3,3,3,256,256]{4,3,2,1,0:T(8,128)(2,1)}, u32[]{:S(2)}) copy-start(bf16[3,3,3,256,256]{4,3,2,1,0:T(8,128)(2,1)} %param.5) | copy-start | bytes 10616836
  7.2 321.6 %reduce-scatter.2.cloned.1.call-start = ((), (), s32[]{:S(2)}) async-start(), calls=%async_computation.1 | async-start | bytes 7520256 | tf_op jit(solution)/shard_map/reduce_scatter | solution.py:101
  11.2 31.0 %collective-permute-start.1 = (bf16[1,256,4,1,128]{4,1,3,2,0:T(8,128)(2,1)}, bf16[1,256,4,1,128]{4,1,3,2,0:T(8,128)(2,1)}, u32[]{:S(2)}, u32[]{:S(2)}) collective-permute-start(bf16[1,256,4,1,128]{4,1,3,2,0:T(8,128)(2,1)} %copy.33), channel_id=1, source_target_pairs={{4,0},{8,4},{12,8},{5,1},{9,5},{13,9},{6,2},{10,6},{14,10},{7,3},{... | collective-permute-start | bytes 786440 | tf_op jit(solution)/shard_map/ppermute | solution.py:22
  13.2 30.3 %collective-permute-start = (bf16[1,256,4,1,128]{4,1,3,2,0:T(8,128)(2,1)}, bf16[1,256,4,1,128]{4,1,3,2,0:T(8,128)(2,1)}, u32[]{:S(2)}, u32[]{:S(2)}) collective-permute-start(bf16[1,256,4,1,128]{4,1,3,2,0:T(8,128)(2,1)} %copy.32), channel_id=1, source_target_pairs={{0,4},{4,8},{8,12},{1,5},{5,9},{9,13},{2,6},{6,10},{10,14},{3,7},{... | collective-permute-start | bytes 786440 | tf_op jit(solution)/shard_map/ppermute | solution.py:20
  229.6 8.8 %copy-start.1 = (bf16[256]{0:T(256)(128)(2,1)S(1)}, bf16[256]{0:T(256)(128)(2,1)}, u32[]{:S(2)}) copy-start(bf16[256]{0:T(256)(128)(2,1)} %param.6) | copy-start | bytes 1540
  229.6 8.8 %copy-start.2 = (u32[32]{0:T(128)S(1)}, u32[32]{0:T(128)}, u32[]{:S(2)}) copy-start(u32[32]{0:T(128)} %constant.19) | copy-start | bytes 388
  238.1 194.7 %all-gather.2.cloned.1.call-start = ((), (), s32[]{:S(2)}) async-start(), calls=%async_computation.2 | async-start | bytes 2211840 | tf_op jit(solution)/shard_map/all_gather | solution.py:102
  286.9 41.9 %copy-start.3 = (pred[8,17]{0,1:T(8,128)(4,1)S(1)}, pred[8,17]{0,1:T(8,128)(4,1)}, u32[]{:S(2)}) copy-start(pred[8,17]{0,1:T(8,128)(4,1)} %constant.16) | copy-start | bytes 412
Sparse Core Ops, SparseCore 0:
  238.2 90.5 reduce-scatter.1
  330.4 20.4 all-gather.1

commit v2 on v1

--- a/solution.py
+++ b/solution.py
@@ -90,21 +90,28 @@
         preferred_element_type=jnp.float32,
     )
     output = (accum + bias.astype(jnp.float32)[None, :, None, None, None]).astype(jnp.bfloat16)
-    wide = jnp.pad(rimmed[0], ((0, 0), (0, 0), (0, 0), (1, 1)))
-    shifts = jnp.stack([wide[..., c : c + width] for c in range(3)])
-    xc = jnp.transpose(shifts, (2, 0, 1, 3, 4)).reshape(depth, 3 * channels, (rows + 2) * width)
+    lanes_h = (rows + 2) * width
+    flat = jnp.transpose(rimmed[0], (1, 0, 2, 3)).reshape(depth, channels, lanes_h)
+    wide = jnp.pad(flat, ((0, 0), (0, 0), (1, 1)))
+    column = lax.broadcasted_iota(jnp.int32, (1, 1, lanes_h), 2) % width
+    zero = jnp.zeros((), flat.dtype)
+    left = jnp.where(column == 0, zero, wide[..., 0:lanes_h])
+    right = jnp.where(column == width - 1, zero, wide[..., 2 : lanes_h + 2])
+    xc = jnp.concatenate([left, flat, right], axis=1)
     gp = cotangent[0].reshape(n_filt, n_patch, piece, depth, rows, width)
     gp = jnp.transpose(gp, (3, 1, 0, 2, 4, 5)).reshape(depth, channels, rows * width)
     grads_all = wgrad(xc, gp)
     grads = jnp.transpose(grads_all.reshape(27 * channels, channels), (1, 0))
     grads = grads.reshape(n_patch * n_filt, piece * 27, channels)
+    bias_all = jnp.sum(cotangent.astype(jnp.float32), axis=(0, 2, 3, 4))
+    bias_all = jnp.transpose(bias_all.reshape(n_filt, n_patch, piece), (1, 0, 2))
+    bias_row = jnp.pad(bias_all.reshape(n_patch * n_filt, 1, piece), ((0, 0), (0, 0), (0, channels - piece)))
+    grads = jnp.concatenate([grads, bias_row], axis=1)
     grads = lax.psum_scatter(grads, ("patch", "filt"), scatter_dimension=0, tiled=True)
     grads = lax.all_gather(grads, "patch", axis=0, tiled=True)
-    grads = grads.reshape(owned, 3, 3, 3, channels)
+    bias_part = grads[:, piece * 27, :piece].reshape(owned)
+    grads = grads[:, : piece * 27, :].reshape(owned, 3, 3, 3, channels)
     filter_grad = jnp.transpose(grads, (1, 2, 3, 4, 0)) * scale
-    bias_all = jnp.sum(cotangent.astype(jnp.float32), axis=(0, 2, 3, 4))
-    bias_part = lax.psum_scatter(bias_all, "filt", scatter_dimension=0, tiled=True)
-    bias_part = lax.psum(bias_part, "patch")
     return (output, filter_grad, bias_part * scale)
 
 

time: 453 us -> 418 us (0.923)
  local copies, waits for them, and re-layouts: 208 us -> 139 us
  waiting for transfers between devices: 30.8 us -> 62.2 us
  other arithmetic: 40.9 us -> 62 us
  blocking collectives: 15.8 us -> 0 us
    reshape x2, local copies, waits for them, and re-layouts: 72.5 us -> 11.8 us  [the longest x1 11.7 us: local(): jnp.transpose(rimmed[0], (1, 0, 2, 3)).reshape(depth, channels, lanes_h)]
    concatenate x0 -> x3, other arithmetic: none -> 35.3 us  [the longest x1 18.7 us: local(): xc = jnp.concatenate([left, flat, right], axis=1)]
    reduce_scatter x1, waiting for transfers between devices: 30.8 us -> 62.2 us  [local(): lax.psum_scatter(grads, ('patch', 'filt'), scatter_dimension=0, tiled=True)]
    transpose x1 -> x0, other arithmetic: 21.2 us -> none  [local(): jnp.transpose(shifts, (2, 0, 1, 3, 4))]
    select_n x0 -> x1, other arithmetic: none -> 18 us  [local(): left = jnp.where(column == 0, zero, wide[..., 0:lanes_h])]
    squeeze x1 -> x0, other arithmetic: 11.3 us -> none  [local(): wide = jnp.pad(rimmed[0], ((0, 0), (0, 0), (0, 0), (1, 1)))]
    unnamed x1 -> x0, blocking collectives: 10.2 us -> none
    another operation x1 -> x0, local copies, waits for them, and re-layouts: 9.91 us -> none  [local(): shifts = jnp.stack([wide[..., c:c + width] for c in range(3)])]
  transfers between devices with their start and end apart: 4 -> 4, of which waited for: 1 -> 1; matrix products, arithmetic and copies ran while one was open for 38% -> 39% of each run, Pallas kernels for 0% -> 0%
where the time goes in v2:
time: 418 us; the launch traced here: 416 us
  local copies, waits for them, and re-layouts  139 us (33%)
  matrix products  70.3 us (17%)
  waiting for transfers between devices  62.2 us (15%)
  other arithmetic  62 us (15%)
  Pallas kernels  61.4 us (15%)
  between operations  14.1 us (3%)
  starting transfers between devices  7.68 us (2%)
    conv_general_dilated x1, matrix products, local(): lax.conv_general_dilated(rimmed, filters, window_strides=(1, 1, 1), paddi...  70.3 us
    reduce_scatter x1, waiting for transfers between devices, local(): lax.psum_scatter(grads, ('patch', 'filt'), scatter_dimension=0, tiled=True)  62.2 us
    pallas_call x1, Pallas kernels, wgrad(): pl.pallas_call(functools.partial(_wgrad_kernel, depth, lanes), grid=(dept...  61.4 us
    unnamed x12, local copies, waits for them, and re-layouts  44.9 us
    concatenate x1, other arithmetic, local(): xc = jnp.concatenate([left, flat, right], axis=1)  18.7 us
    select_n x1, other arithmetic, local(): left = jnp.where(column == 0, zero, wide[..., 0:lanes_h])  18 us
    convert_element_type x2, local copies, waits for them, and re-layouts, local(): (accum + bias.astype(jnp.float32)[None, :, None, None, None]).astype(jnp....  16.7 us
    reshape x1, local copies, waits for them, and re-layouts, local(): jnp.transpose(gp, (3, 1, 0, 2, 4, 5)).reshape(depth, channels, rows * width)  13.3 us
  transfers between devices with their start and end apart: 4, of which 1 were waited for; matrix products, arithmetic and copies ran while one was open for 39% of the time, Pallas kernels for 0%

profile of v2, /device:TPU:0, one launch (start us, length us, event | category | flops | bytes accessed | tf_op | source)
XLA Modules:
  0.0 416.1 jit_solution(10481467673315696614)
XLA Ops:
  7.2 0.0 copy-start
  7.2 0.0 reduce-scatter.2.cloned.1.call-start
  7.2 13.9 %copy.23 = bf16[1,256,4,32,128]{1,4,3,2,0:T(8,128)(2,1)} copy(bf16[1,256,4,32,128]{4,3,2,1,0:T(8,128)(2,1)} %param.4) | data formatting | bytes 16777216 | tf_op args[0]
  21.1 1.9 fusion.21
  23.0 1.3 collective-permute-start.1
  24.2 6.3 %collective-permute-start = (bf16[1,256,4,1,128]{1,4,3,2,0:T(8,128)(2,1)}, bf16[1,256,4,1,128]{1,4,3,2,0:T(8,128)(2,1)}, u32[]{:S(2)}, u32[]{:S(2)}) collective-permute-start(bf16[1,256,4,1,128]{1,4,3,2,0:T(8,128)(2,1)} %get-tuple-element.13), channel_id=1, source_target_pairs={{0,4},{4,8},{8,12},{1,5},{5,9},{9,13},{2,6},{6,10},{10,14},{3,7},{... | collective-permute-start | bytes 786440 | tf_op jit(solution)/shard_map/ppermute | solution.py:20
  30.6 5.0 %convert_reduce_fusion = f32[256]{0:T(256)S(1)} fusion(bf16[1,256,4,32,128]{4,3,2,1,0:T(8,128)(2,1)} %param.7), kind=kLoop, calls=%fused_computation.4 | loop fusion | flops 8388352 | bytes 8389632 | tf_op jit(solution)/shard_map/reduce_sum | solution.py:106
  35.6 0.1 reshape.56
  35.7 0.6 copy.34
  36.3 9.2 %copy.39 = bf16[4,4,16,4,32,128]{5,4,2,0,1,3:T(8,128)(2,1)} copy(bf16[4,4,16,4,32,128]{5,4,3,2,1,0:T(8,128)(2,1)} %bitcast.34) | data formatting | bytes 16777216 | tf_op jit(solution)/shard_map/reshape;squeeze | solution.py:101
  45.5 13.3 %reshape.53.g_ref = bf16[4,256,4096]{2,1,0:T(8,128)(2,1)} reshape(bf16[4,4,4,16,32,128]{5,4,3,2,1,0:T(8,128)(2,1)} %bitcast.35) | data formatting | bytes 16777216 | tf_op jit(solution)/shard_map/reshape | solution.py:102
  58.8 0.0 collective-permute-done.1
  58.8 0.0 collective-permute-done
  58.8 10.0 %pad_maximum_fusion.1 = (bf16[1,256,4,34,128]{1,4,3,2,0:T(8,128)(2,1)}, bf16[256,4,34,1,128]{0,4,2,1,3:T(8,128)(2,1)}) fusion(bf16[1,256,4,1,128]{1,4,3,2,0:T(8,128)(2,1)} %collective-permute-done.1, bf16[1,256,4,32,128]{1,4,3,2,0:T(8,128)(2,1)} %copy.23, bf16[1,256,4,1,128]{1,4,3,2,0:T(8,128)(2,1)} %collective-permute-done), kind=kLoop, calls=%fused_computation.11 | loop fusion | flops 8912896 | bytes 26738688 | tf_op jit(solution)/shard_map/concatenate | solution.py:18
  68.9 11.7 %copy.30 = bf16[4,256,4352]{2,1,0:T(8,128)(2,1)} copy(bf16[4,256,4352]{1,2,0:T(8,128)(2,1)} %bitcast.32) | data formatting | bytes 17825792 | tf_op jit(solution)/shard_map/reshape | solution.py:94
  80.6 18.0 %slice_select_fusion.1 = (bf16[4,256,4352]{2,1,0:T(8,128)(2,1)}, bf16[4,256,4352]{2,1,0:T(8,128)(2,1)}) fusion(pred[4352]{0:T(1024)(128)(4,1)S(1)} %get-tuple-element.16, bf16[4,256,4352]{2,1,0:T(8,128)(2,1)} %copy.30, pred[4352]{0:T(1024)(128)(4,1)S(1)} %get-tuple-element.15), kind=kLoop, calls=%fused_computation.13 | loop fusion | flops 8912896 | bytes 26747392 | tf_op jit(solution)/shard_map/jit(_where)/select_n | solution.py:98
  98.6 18.7 %pad_maximum_fusion.x_ref = bf16[4,768,4352]{2,1,0:T(8,128)(2,1)} fusion(bf16[4,256,4352]{2,1,0:T(8,128)(2,1)} %get-tuple-element.10, bf16[4,256,4352]{2,1,0:T(8,128)(2,1)} %copy.30, bf16[4,256,4352]{2,1,0:T(8,128)(2,1)} %get-tuple-element.9), kind=kLoop, calls=%fused_computation | loop fusion | flops 80216064 | bytes 53477376 | tf_op jit(solution)/shard_map/concatenate | solution.py:100
  117.3 61.4 %shard_map.67 = f32[3,3,768,256]{3,2,1,0:T(8,128)} custom-call(bf16[4,768,4352]{2,1,0:T(8,128)(2,1)} %pad_maximum_fusion.x_ref, bf16[4,256,4096]{2,1,0:T(8,128)(2,1)} %reshape.53.g_ref), custom_call_target="tpu_custom_call" | custom-call | flops 173946175488 | bytes 58982400 | tf_op jit(solution)/shard_map/pallas_call | solution.py:56
  178.7 8.5 %copy.33 = f32[6912,256]{0,1:T(8,128)} copy(f32[6912,256]{1,0:T(8,128)} %bitcast.38) | data formatting | bytes 14155776 | tf_op jit(solution)/shard_map/reshape | solution.py:104
  187.1 0.0 copy-start.1
  187.2 8.5 %reshape.55 = f32[16,432,256]{2,1,0:T(8,128)} reshape(f32[256,6912]{1,0:T(8,128)} %bitcast.36) | data formatting | bytes 14155776 | tf_op jit(solution)/shard_map/reshape | solution.py:105
  195.6 0.0 copy-done.1
  195.6 0.0 copy-start.2
  195.6 6.6 %select_maximum_fusion = f32[16,433,256]{2,1,0:T(8,128)} fusion(f32[16,1,16]{2,1,0:T(1,128)S(1)} %bitcast.39, f32[16,432,256]{2,1,0:T(8,128)} %reshape.55), kind=kLoop, calls=%fused_computation.16 | loop fusion | flops 5320704 | bytes 14173184 | tf_op jit(solution)/shard_map/concatenate | solution.py:109
  202.3 0.0 reduce-scatter.2.cloned.1.call-update
  202.3 0.0 all-gather.2.cloned.1.call-start
  202.3 0.0 copy-done.2
  202.3 11.0 %copy.37 = bf16[256,4,34,1,128]{0,1,4,2,3:T(4,128)(2,1)S(1)} copy(bf16[256,4,34,1,128]{0,4,2,1,3:T(8,128)(2,1)} %get-tuple-element.12) | data formatting | bytes 17825792
  213.3 6.7 %pad.10.clone = bf16[256,4,34,1,136]{0,1,4,2,3:T(4,128)(2,1)} pad(bf16[256,4,34,1,128]{0,1,4,2,3:T(4,128)(2,1)S(1)} %copy.37, bf16[]{:T(256)} %constant.25.clone.1), padding=0_0x0_0x0_0x0_0x1_7 | pad | bytes 18382850 | tf_op jit(solution)/shard_map/concatenate | solution.py:18
  220.0 0.0 copy-start.3
  220.0 9.4 %copy.28 = bf16[256,4,34,1,8,17]{0,4,5,2,1,3:T(8,128)(2,1)} copy(bf16[256,4,34,1,8,17]{0,1,5,4,2,3:T(4,128)(2,1)} %bitcast.31) | data formatting | bytes 18939904 | tf_op jit(solution)/shard_map/conv_general_dilated | solution.py:84
  229.4 2.5 slice.28
  231.9 62.2 %reduce-scatter.2.cloned.1.call-done = f32[1,433,256]{2,1,0:T(8,128)} async-done(((f32[16,433,256]{2,1,0:T(8,128)}), f32[1,433,256]{2,1,0:T(8,128)}) %reduce-scatter.2.cloned.1.call-update) | async-done | bytes 443408 | tf_op jit(solution)/shard_map/reduce_scatter | solution.py:110
  294.1 0.0 all-gather.2.cloned.1.call-update
  294.1 0.0 copy-done
  294.1 0.0 copy-done.3
  294.1 70.3 %add_convert_fusion = bf16[4,32,8,17,256]{4,2,3,1,0:T(8,128)(2,1)} fusion(f32[256]{0:T(256)S(1)} %convert_element_type.13, pred[8,17]{0,1:T(8,128)(4,1)S(1)} %copy-done.3, bf16[3,3,3,256,256]{4,3,2,1,0:T(8,128)(2,1)S(1)} %copy-done, bf16[256,4,34,1,7,2]{0,4,5,2,1,3:T(8,128)(2,1)} %slice.28, bf16[256,4,34,1,8,17]{0,4,5,2,1,3:T(8,128)(2,1)} %copy.28), kind=kOutput, calls=%fused_computation.3 | convolution fusion | flops 51383402496 | bytes 22897800 | tf_op jit(solution)/shard_map/conv_general_dilated | solution.py:84
  364.4 9.1 %copy.29 = bf16[4,32,8,17,256]{4,1,3,2,0:T(8,128)(2,1)} copy(bf16[4,32,8,17,256]{4,2,3,1,0:T(8,128)(2,1)} %add_convert_fusion) | data formatting | bytes 17825792 | tf_op jit(solution)/shard_map/convert_element_type | solution.py:92
  373.5 7.6 %slice_bitcast_fusion = bf16[1,256,4,32,128]{1,3,4,2,0:T(8,128)(2,1)} fusion(bf16[4,32,1,136,256]{4,1,3,0,2:T(8,128)(2,1)} %bitcast.33), kind=kLoop, calls=%fused_computation.14 | loop fusion | bytes 16777216 | tf_op jit(solution)/shard_map/convert_element_type | solution.py:92
  381.1 16.9 %copy.35 = bf16[1,256,4,32,128]{4,3,2,1,0:T(8,128)(2,1)} copy(bf16[1,256,4,32,128]{1,3,4,2,0:T(8,128)(2,1)} %slice_bitcast_fusion) | data formatting | bytes 16777216
  398.0 0.0 all-gather.2.cloned.1.call-done
  398.0 2.8 slice_multiply_fusion
  400.8 3.9 mul.23
  404.8 3.2 copy.36
  408.0 0.7 fusion.16
  408.7 0.6 mul.27
  (2 shorter events, 0.0 us)
Async XLA Ops:
  7.2 286.9 %copy-start = (bf16[3,3,3,256,256]{4,3,2,1,0:T(8,128)(2,1)S(1)}, bf16[3,3,3,256,256]{4,3,2,1,0:T(8,128)(2,1)}, u32[]{:S(2)}) copy-start(bf16[3,3,3,256,256]{4,3,2,1,0:T(8,128)(2,1)} %param.5) | copy-start | bytes 10616836
  7.2 286.9 %reduce-scatter.2.cloned.1.call-start = ((), (), s32[]{:S(2)}) async-start(), calls=%async_computation.1 | async-start | bytes 7659520 | tf_op jit(solution)/shard_map/reduce_scatter | solution.py:110
  23.0 35.9 %collective-permute-start.1 = (bf16[1,256,4,1,128]{1,4,3,2,0:T(8,128)(2,1)}, bf16[1,256,4,1,128]{1,4,3,2,0:T(8,128)(2,1)}, u32[]{:S(2)}, u32[]{:S(2)}) collective-permute-start(bf16[1,256,4,1,128]{1,4,3,2,0:T(8,128)(2,1)} %get-tuple-element.14), channel_id=1, source_target_pairs={{4,0},{8,4},{12,8},{5,1},{9,5},{13,9},{6,2},{10,6},{14,10},{7,3},{... | collective-permute-start | bytes 786440 | tf_op jit(solution)/shard_map/ppermute | solution.py:22
  24.2 34.6 %collective-permute-start = (bf16[1,256,4,1,128]{1,4,3,2,0:T(8,128)(2,1)}, bf16[1,256,4,1,128]{1,4,3,2,0:T(8,128)(2,1)}, u32[]{:S(2)}, u32[]{:S(2)}) collective-permute-start(bf16[1,256,4,1,128]{1,4,3,2,0:T(8,128)(2,1)} %get-tuple-element.13), channel_id=1, source_target_pairs={{0,4},{4,8},{8,12},{1,5},{5,9},{9,13},{2,6},{6,10},{10,14},{3,7},{... | collective-permute-start | bytes 786440 | tf_op jit(solution)/shard_map/ppermute | solution.py:20
  187.1 8.5 %copy-start.1 = (f32[4,4,16]{2,1,0:T(4,128)S(1)}, f32[4,4,16]{2,1,0:T(4,128)}, u32[]{:S(2)}) copy-start(f32[4,4,16]{2,1,0:T(4,128)} %copy.34) | copy-start | bytes 3076
  195.6 6.7 %copy-start.2 = (bf16[256]{0:T(256)(128)(2,1)S(1)}, bf16[256]{0:T(256)(128)(2,1)}, u32[]{:S(2)}) copy-start(bf16[256]{0:T(256)(128)(2,1)} %param.6) | copy-start | bytes 1540
  202.3 195.7 %all-gather.2.cloned.1.call-start = ((), (), s32[]{:S(2)}) async-start(), calls=%async_computation.2 | async-start | bytes 2252800 | tf_op jit(solution)/shard_map/all_gather | solution.py:111
  220.0 74.1 %copy-start.3 = (pred[8,17]{0,1:T(8,128)(4,1)S(1)}, pred[8,17]{0,1:T(8,128)(4,1)}, u32[]{:S(2)}) copy-start(pred[8,17]{0,1:T(8,128)(4,1)} %constant.38) | copy-start | bytes 412
Sparse Core Ops, SparseCore 0:
  202.4 91.6 reduce-scatter.1
  295.6 20.5 all-gather.1
